TPU v7x, 256 devices: a whole 4x4x8 slice. The times are simulated.
256 devices in a mesh: req: 128 (over y_hi, z, x, core), tp: 2 (over y_lo).
Axes of the slice: x: 4, y: 4 (y_hi: 2, y_lo: 2; y = y_hi * 2 + y_lo), z: 8, core: 2. Of those that a mesh axis runs over, the one named last changes fastest.
Arguments:
- tokens: bfloat16 [256, 512, 2048], P('req'), may hold values from -6 to 6
- qkv_master: float32 [2048, 3, 2048], P('req', None, 'tp')
- q_gain: float32 [2048], P('tp')
- k_gain: float32 [2048], P('tp')
- lengths: int32 [256], P('req'), may hold values from 1 to 512, as said below
- page_holder: int32 [256, 4], P('req'), may hold values from 0 to 127, as said below
- page_slot: int32 [256, 4], P('req'), may hold values from 0 to 2, as said below
Outputs:
- attended: bfloat16 [256, 512, 2048], P('req', None, 'tp')
- kv_cache: bfloat16 [1152, 2, 128, 2048], P('req', None, None, 'tp')
Inputs may be any that keep to these rules, and one draw needn't show every extreme that they name: lengths[r] is at least 1; some prompt has exactly 512 tokens. page_holder[r, p] is r // 2, or the index just before or just after it along req, cyclically. The live pages of one req index's prompts that go to one holder have distinct page_slot values, so at most 3 of them; some req index sends 3 live pages to one holder.
All inputs are finite; a program needn't handle non-finite values.
Results may differ from a plain program's by a relative error of at most 0.009.
Values may be sent and summed in bfloat16 or wider, within the bound.
No kernel may reach another device: no remote copies, remote signals or barrier semaphores. Data moves between devices by JAX's collectives and lax.ppermute only.
A program may use at most 128 MiB of HBM per device.

v0:
```python
import jax
import jax.numpy as jnp
from jax import lax
from jax.sharding import PartitionSpec as P

HD = 128
PAGE = 128
CAP = 3
SLOTS = 9
norm_epsilon = 1e-06
rope_theta = 500000.0


def extended(block, sides, width):
    for axis, dim in sides:
        count = lax.axis_size(axis)
        forward = [(i, i + 1) for i in range(count - 1)]
        forward.append((count - 1, 0))
        backward = [(target, source) for source, target in forward]
        low = lax.ppermute(
            lax.slice_in_dim(block, block.shape[dim] - width, None, axis=dim), axis, forward
        )
        high = lax.ppermute(lax.slice_in_dim(block, 0, width, axis=dim), axis, backward)
        block = jnp.concatenate([low, block, high], axis=dim)
    return block


def rotate(values_in, seq_len, head_size):
    half_size = head_size // 2
    positions = jnp.arange(seq_len).astype(jnp.float32)
    frequency = rope_theta ** (-jnp.arange(half_size).astype(jnp.float32) * 2.0 / head_size)
    angles = positions[:, None] * frequency[None, :]
    cosine_table = jnp.cos(angles)[:, None, :]
    sine_table = jnp.sin(angles)[:, None, :]
    front_half = values_in[..., :half_size]
    back_half = values_in[..., half_size:]
    return jnp.concatenate(
        [
            front_half * cosine_table - back_half * sine_table,
            back_half * cosine_table + front_half * sine_table,
        ],
        -1,
    )


def attend(request_item):
    queries, key_rows, value_rows, length = request_item
    seq_len = queries.shape[0]
    scores = jnp.einsum(
        "thd,uhd->htu", queries, key_rows, preferred_element_type=jnp.float32
    ) * HD ** (-0.5)
    query_pos = jnp.arange(seq_len)[:, None]
    key_pos = jnp.arange(seq_len)[None, :]
    allowed = (key_pos <= query_pos) & (key_pos < length)
    scores = jnp.where(allowed[None], scores, -1e30)
    row_max = jnp.max(scores, axis=-1, keepdims=True)
    exp_terms = jnp.where(allowed[None], jnp.exp(scores - row_max), 0.0)
    probs = (exp_terms / jnp.sum(exp_terms, axis=-1, keepdims=True)).astype(jnp.bfloat16)
    output = jnp.einsum("htu,uhd->thd", probs, value_rows, preferred_element_type=jnp.float32)
    keep_rows = jnp.arange(seq_len)[:, None, None] < length
    return jnp.where(keep_rows, output, 0.0).astype(jnp.bfloat16)


def body(tokens, qkv_master, q_gain, k_gain, lengths, page_holder, page_slot):
    req_dev, seq_len, model_width = tokens.shape
    row_share, _, q_local = qkv_master.shape
    heads_local = q_local // HD
    token_rows = tokens.reshape(req_dev * seq_len, model_width)
    master_local = qkv_master.astype(jnp.bfloat16).reshape(row_share, 3 * q_local)
    gathered = lax.all_gather(master_local, "req", axis=0, tiled=True)
    projected = jnp.dot(token_rows, gathered, preferred_element_type=jnp.float32)
    queries = projected[:, :q_local]
    key_rows = projected[:, q_local : 2 * q_local]
    values = projected[:, 2 * q_local :]
    square_sums = lax.psum((jnp.sum(queries * queries, -1), jnp.sum(key_rows * key_rows, -1)), "tp")
    full_width = q_local * lax.axis_size("tp")
    queries = queries * lax.rsqrt(square_sums[0] / full_width + norm_epsilon)[:, None] * q_gain
    key_rows = key_rows * lax.rsqrt(square_sums[1] / full_width + norm_epsilon)[:, None] * k_gain
    q_rot = rotate(queries.reshape(req_dev, seq_len, heads_local, HD), seq_len, HD).astype(
        jnp.bfloat16
    )
    k_rot = rotate(key_rows.reshape(req_dev, seq_len, heads_local, HD), seq_len, HD).astype(
        jnp.bfloat16
    )
    v_round = values.astype(jnp.bfloat16).reshape(req_dev, seq_len, heads_local, HD)
    attended = lax.map(attend, (q_rot, k_rot, v_round, lengths)).reshape(req_dev, seq_len, q_local)
    page_count = seq_len // PAGE
    home_index = lax.axis_index("req")
    axis_count = lax.axis_size("req")
    is_live = (jnp.arange(page_count) * PAGE)[None, :] < lengths[:, None]
    offset = (page_holder - home_index + 1 + axis_count) % axis_count - 1
    target = jnp.where(is_live, (offset + 1) * CAP + page_slot, -1).reshape(-1)
    onehot = (target[None, :] == jnp.arange(SLOTS)[:, None]).astype(jnp.bfloat16)
    stacked = jnp.stack(
        [
            k_rot.reshape(req_dev * page_count, PAGE * q_local),
            v_round.reshape(req_dev * page_count, PAGE * q_local),
        ],
        1,
    )
    stacked = stacked.reshape(req_dev * page_count, 2 * PAGE * q_local)
    outgoing = (
        jnp.dot(onehot, stacked, preferred_element_type=jnp.float32)
        .astype(jnp.bfloat16)
        .reshape(SLOTS, 2, PAGE, q_local)
    )
    padded = extended(outgoing, (("req", 0),), CAP)
    kv_cache = jnp.concatenate([padded[CAP + SLOTS :], outgoing[CAP : 2 * CAP], padded[:CAP]], 0)
    return (attended, kv_cache)


def solution(mesh):
    in_specs = (
        P("req", None, None),
        P("req", None, "tp"),
        P("tp"),
        P("tp"),
        P("req"),
        P("req", None),
        P("req", None),
    )
    out_specs = (P("req", None, "tp"), P("req", None, None, "tp"))
    return jax.shard_map(body, mesh=mesh, in_specs=in_specs, out_specs=out_specs, check_vma=False)
```

profile of v0, /device:TPU:8, one launch (start us, length us, event | category | flops | bytes accessed | tf_op | source)
XLA Modules:
  0.0 286.8 jit_solution(13818143167871856922)
XLA Ops:
  7.2 0.9 convert_bitcast_fusion
  8.2 0.6 copy.32
  8.9 0.8 compare_select_fusion.2
  9.7 1.0 multiply_cosine_fusion
  10.7 142.0 %all-gather.2.cloned.1.call-done = bf16[2048,3072]{1,0:T(8,128)(2,1)} async-done(((bf16[16,3072]{1,0:T(8,128)(2,1)}), bf16[2048,3072]{1,0:T(8,128)(2,1)}) %all-gather.2.cloned.1.call-update) | async-done | bytes 12582928 | tf_op jit(solution)/shard_map/all_gather | solution.py:70
  152.7 17.0 %fusion.26 = f32[1024,3072]{1,0:T(8,128)S(1)} fusion(bf16[1024,2048]{1,0:T(8,128)(2,1)} %bitcast.68, bf16[2048,3072]{1,0:T(8,128)(2,1)} %all-gather.2.cloned.1.call-done), kind=kOutput, calls=%fused_computation.61 | convolution fusion | flops 12884901888 | bytes 29360128 | tf_op jit(solution)/shard_map/dot_general | solution.py:71
  169.7 0.6 multiply_reduce_fusion
  170.8 3.4 %copy-done.1 = f32[1024,3072]{1,0:T(8,128)} copy-done((f32[1024,3072]{1,0:T(8,128)}, f32[1024,3072]{1,0:T(8,128)S(1)}, u32[]{:S(2)}) %copy-start.1) | copy-done | bytes 12582936
  174.6 1.9 copy.33
  176.5 5.0 %all-reduce = (f32[1024]{0:T(1024)S(1)}, f32[1024]{0:T(1024)S(1)}) all-reduce(f32[1024]{0:T(1024)S(1)} %get-tuple-element.48, f32[1024]{0:T(1024)S(1)} %get-tuple-element.47), channel_id=1, replica_groups=mesh['req'=128,'tp'=2] {'tp'}, use_global_device_ids=true, to_apply=%region_1.0 | all-reduce | flops 2048 | bytes 16384 | tf_op jit(solution)/shard_map/psum | solution.py:75
  181.5 5.3 %multiply_bitcast_fusion = (f32[128,8,8,128]{3,1,2,0:T(8,128)S(1)}, f32[128,8,8,128]{3,1,2,0:T(8,128)}) fusion(f32[1024,3072]{1,0:T(8,128)} %copy-done.1, f32[1024]{0:T(1024)S(1)} %copy-done.8, f32[1024]{0:T(1024)S(1)} %get-tuple-element.80, f32[1024]{0:T(1024)S(1)} %copy-done.9, f32[1024]{0:T(1024)S(1)} %get-tuple-element.81), kind=kLoop, calls=%fused_computation.32 | loop fusion | flops 4194304 | bytes 16793600
  186.8 3.0 %copy.35 = f32[128,8,8,128]{3,2,1,0:T(8,128)} copy(f32[128,8,8,128]{3,1,2,0:T(8,128)S(1)} %get-tuple-element.65) | data formatting | bytes 8388608
  189.7 2.3 stack_reshape_reshape.3
  192.0 3.2 %copy.34 = f32[128,8,8,128]{3,2,1,0:T(8,128)S(1)} copy(f32[128,8,8,128]{3,1,2,0:T(8,128)} %get-tuple-element.66) | data formatting | bytes 8388608
  195.2 4.7 %fusion.25 = (f32[2,512,8,64]{3,2,1,0:T(8,128)}, f32[2,512,8,64]{3,2,1,0:T(8,128)}) fusion(f32[2,512,8,128]{3,2,1,0:T(8,128)S(1)} %bitcast.59), kind=kLoop, calls=%fused_computation.59 | loop fusion | bytes 8388608 | tf_op jit(solution)/shard_map/slice | solution.py:35
  199.9 1.3 fusion.24
  201.3 1.7 multiply_subtract_fusion
  202.9 1.2 maximum_convert_fusion
  204.1 2.7 copy.24
  206.8 3.8 %convert_element_type.79 = bf16[8,1,131072]{2,0,1:T(8,128)(2,1)} reshape(bf16[2,512,8,128]{3,2,1,0:T(8,128)(2,1)} %copy.24) | data formatting | bytes 4194304 | tf_op jit(solution)/shard_map/convert_element_type | solution.py:82
  210.6 2.6 pad_maximum_fusion.1
  213.2 2.6 convolution_convert_fusion
  215.8 3.5 %fusion.23 = (bf16[3,262144]{1,0:T(4,128)(2,1)S(1)}, bf16[3,262144]{1,0:T(4,128)(2,1)S(1)}, bf16[3,262144]{1,0:T(4,128)(2,1)}) fusion(bf16[9,262144]{1,0:T(8,128)(2,1)S(1)} %convolution_convert_fusion), kind=kLoop, calls=%fused_computation.57 | loop fusion | bytes 9437184 | tf_op jit(solution)/shard_map/slice | solution.py:23
  219.3 1.8 copy.36
  221.0 1.8 copy.38
  222.8 7.5 %collective-permute-start = (bf16[3,2,128,1024]{3,2,1,0:T(8,128)(2,1)}, bf16[3,2,128,1024]{3,2,1,0:T(8,128)(2,1)}, u32[]{:S(2)}, u32[]{:S(2)}) collective-permute-start(bf16[3,2,128,1024]{3,2,1,0:T(8,128)(2,1)} %bitcast.24), channel_id=1, source_target_pairs={{2,0},{4,2},{6,4},{8,6},{10,8},{12,10},{14,12},{16,14},{18,16},{20... | collective-permute-start | bytes 4718600 | tf_op jit(solution)/shard_map/ppermute | solution.py:23
  230.3 1.7 subtract_convert_fusion
  232.0 2.5 pad_maximum_fusion.2
  234.4 37.0 %while.10 = (s32[]{:T(128)}, bf16[2,512,8,128]{1,3,2,0:T(8,128)(2,1)}, s32[2]{0:T(128)S(1)}, bf16[2,512,8,128]{3,2,1,0:T(8,128)(2,1)}, bf16[2,512,8,128]{3,1,2,0...) while((s32[]{:T(128)}, bf16[2,512,8,128]{1,3,2,0:T(8,128)(2,1)}, s32[2]{0:T(128)S(1)}, ...), condition=%wide.region_7.8_spmd, body=%wide.region_4.7_spmd.sunk | while | flops 1094190080 | bytes 63474368 | solution.py:86
  234.4 0.6 dynamic_slice.30
  235.0 0.6 iota_compare_fusion.5
  235.8 1.3 constant_dynamic-slice_fusion.2
  237.1 1.5 copy.48
  238.6 2.5 fusion.40
  241.1 6.3 %fusion.42 = (f32[8,512]{1,0:T(8,128)S(1)}, f32[8,512,512]{1,2,0:T(8,128)}) fusion(f32[8,512,512]{1,2,0:T(8,128)S(1)} %fusion.40, pred[512,512]{0,1:T(8,128)(4,1)S(1)} %fusion.41), kind=kOutput, calls=%fused_computation.56.clone.1 | output fusion | flops 14680575 | bytes 17055744 | tf_op jit(solution)/shard_map/while/body/eval_jaxpr/sub | solution.py:57
  247.4 4.2 %fusion.43 = bf16[2,512,8,128]{1,3,2,0:T(8,128)(2,1)S(1)} fusion(bf16[2,512,8,128]{1,3,2,0:T(8,128)(2,1)S(1)} %copy-done.6, s32[]{:T(128)S(6)} %copy.52, f32[8,512,512]{1,2,0:T(8,128)} %get-tuple-element.121, f32[8,512]{1,0:T(8,128)S(1)} %get-tuple-element.122, bf16[1,512,8,128]{1,3,2,0:T(8,128)(2,1)S(1)} %copy-done.2, ...), kind=kOutput, calls=%fused_computation.11.clone.1 | convolution fusion | flops 542113792 | bytes 10502660 | tf_op jit(solution)/shard_map/while/body/eval_jaxpr/htu,uhd->thd/dot_general | solution.py:59
  251.6 1.3 copy-done.7
  252.9 0.6 dynamic_slice.30
  253.5 0.6 iota_compare_fusion.5
  254.3 1.3 constant_dynamic-slice_fusion.2
  255.6 1.5 copy.48
  257.1 2.5 fusion.40
  259.6 6.3 %fusion.42 = (f32[8,512]{1,0:T(8,128)S(1)}, f32[8,512,512]{1,2,0:T(8,128)}) fusion(f32[8,512,512]{1,2,0:T(8,128)S(1)} %fusion.40, pred[512,512]{0,1:T(8,128)(4,1)S(1)} %fusion.41), kind=kOutput, calls=%fused_computation.56.clone.1 | output fusion | flops 14680575 | bytes 17055744 | tf_op jit(solution)/shard_map/while/body/eval_jaxpr/sub | solution.py:57
  265.9 4.2 %fusion.43 = bf16[2,512,8,128]{1,3,2,0:T(8,128)(2,1)S(1)} fusion(bf16[2,512,8,128]{1,3,2,0:T(8,128)(2,1)S(1)} %copy-done.6, s32[]{:T(128)S(6)} %copy.52, f32[8,512,512]{1,2,0:T(8,128)} %get-tuple-element.121, f32[8,512]{1,0:T(8,128)S(1)} %get-tuple-element.122, bf16[1,512,8,128]{1,3,2,0:T(8,128)(2,1)S(1)} %copy-done.2, ...), kind=kOutput, calls=%fused_computation.11.clone.1 | convolution fusion | flops 542113792 | bytes 10502660 | tf_op jit(solution)/shard_map/while/body/eval_jaxpr/htu,uhd->thd/dot_general | solution.py:59
  270.1 1.3 copy-done.7
  271.4 4.1 %copy.26 = bf16[2,512,1024]{2,1,0:T(8,128)(2,1)} copy(bf16[2,512,1024]{1,2,0:T(8,128)(2,1)} %bitcast.66) | data formatting | bytes 4194304 | tf_op jit(solution)/shard_map/reshape | solution.py:86
  275.5 0.6 copy.37
  276.1 3.8 %pad_maximum_fusion = bf16[9,2,128,1024]{3,2,1,0:T(8,128)(2,1)} fusion(bf16[3,2,128,1024]{3,2,1,0:T(8,128)(2,1)} %collective-permute-done.1, bf16[3,2,128,1024]{3,2,1,0:T(8,128)(2,1)S(1)} %bitcast.65, bf16[3,2,128,1024]{3,2,1,0:T(8,128)(2,1)} %collective-permute-done), kind=kLoop, calls=%fused_computation.26 | loop fusion | flops 4718592 | bytes 9437184 | tf_op jit(solution)/shard_map/concatenate | solution.py:108
  (40 shorter events, 1.3 us)
Async XLA Ops:
  7.2 145.5 %all-gather.2.cloned.1.call-start = ((), (), s32[]{:S(2)}) async-start(), calls=%async_computation | async-start | bytes 12681216 | tf_op jit(solution)/shard_map/all_gather | solution.py:70
  169.7 4.6 %copy-start.1 = (f32[1024,3072]{1,0:T(8,128)}, f32[1024,3072]{1,0:T(8,128)S(1)}, u32[]{:S(2)}) copy-start(f32[1024,3072]{1,0:T(8,128)S(1)} %fusion.26) | copy-start | bytes 37748740
  174.2 7.3 %copy-start.8 = (f32[1024]{0:T(1024)S(1)}, f32[1024]{0:T(1024)}, u32[]{:S(2)}) copy-start(f32[1024]{0:T(1024)} %param.12) | copy-start | bytes 12292
  174.2 7.3 %copy-start.9 = (f32[1024]{0:T(1024)S(1)}, f32[1024]{0:T(1024)}, u32[]{:S(2)}) copy-start(f32[1024]{0:T(1024)} %param.11) | copy-start | bytes 12292
  195.2 4.7 %copy-start = (f32[128,8,8,128]{3,2,1,0:T(8,128)S(1)}, f32[128,8,8,128]{3,2,1,0:T(8,128)}, u32[]{:S(2)}) copy-start(f32[128,8,8,128]{3,2,1,0:T(8,128)} %copy.35) | copy-start | bytes 12582916
  215.8 14.5 %copy-start.4 = (f32[2,512,8,64]{3,2,1,0:T(8,128)S(1)}, f32[2,512,8,64]{3,2,1,0:T(8,128)}, u32[]{:S(2)}) copy-start(f32[2,512,8,64]{3,2,1,0:T(8,128)} %get-tuple-element.77) | copy-start | bytes 6291460
  219.3 11.0 %copy-start.3 = (f32[2,512,8,64]{3,2,1,0:T(8,128)S(1)}, f32[2,512,8,64]{3,2,1,0:T(8,128)}, u32[]{:S(2)}) copy-start(f32[2,512,8,64]{3,2,1,0:T(8,128)} %get-tuple-element.76) | copy-start | bytes 6291460
  222.8 53.3 %collective-permute-start.1 = (bf16[3,2,128,1024]{3,2,1,0:T(8,128)(2,1)}, bf16[3,2,128,1024]{3,2,1,0:T(8,128)(2,1)}, u32[]{:S(2)}, u32[]{:S(2)}) collective-permute-start(bf16[3,2,128,1024]{3,2,1,0:T(8,128)(2,1)} %bitcast.30), channel_id=1, source_target_pairs={{0,2},{2,4},{4,6},{6,8},{8,10},{10,12},{12,14},{14,16},{16,18},{18... | collective-permute-start | bytes 4718600 | tf_op jit(solution)/shard_map/ppermute | solution.py:20
  222.8 53.3 %collective-permute-start = (bf16[3,2,128,1024]{3,2,1,0:T(8,128)(2,1)}, bf16[3,2,128,1024]{3,2,1,0:T(8,128)(2,1)}, u32[]{:S(2)}, u32[]{:S(2)}) collective-permute-start(bf16[3,2,128,1024]{3,2,1,0:T(8,128)(2,1)} %bitcast.24), channel_id=1, source_target_pairs={{2,0},{4,2},{6,4},{8,6},{10,8},{12,10},{14,12},{16,14},{18,16},{20... | collective-permute-start | bytes 4718600 | tf_op jit(solution)/shard_map/ppermute | solution.py:23
  231.9 2.5 copy-start.10
  241.1 6.3 %copy-start.2 = (bf16[1,512,8,128]{1,3,2,0:T(8,128)(2,1)S(1)}, bf16[1,512,8,128]{1,3,2,0:T(8,128)(2,1)}, u32[]{:S(2)}) copy-start(bf16[1,512,8,128]{1,3,2,0:T(8,128)(2,1)} %copy.48) | copy-start | bytes 3145732 | tf_op jit(solution)/shard_map/while
  241.1 6.3 %copy-start.6 = (bf16[2,512,8,128]{1,3,2,0:T(8,128)(2,1)S(1)}, bf16[2,512,8,128]{1,3,2,0:T(8,128)(2,1)}, u32[]{:S(2)}) copy-start(bf16[2,512,8,128]{1,3,2,0:T(8,128)(2,1)} %get-tuple-element.131) | copy-start | bytes 6291460 | tf_op jit(solution)/shard_map/while
  251.6 1.3 copy-start.7
  259.6 6.3 %copy-start.2 = (bf16[1,512,8,128]{1,3,2,0:T(8,128)(2,1)S(1)}, bf16[1,512,8,128]{1,3,2,0:T(8,128)(2,1)}, u32[]{:S(2)}) copy-start(bf16[1,512,8,128]{1,3,2,0:T(8,128)(2,1)} %copy.48) | copy-start | bytes 3145732 | tf_op jit(solution)/shard_map/while
  259.6 6.3 %copy-start.6 = (bf16[2,512,8,128]{1,3,2,0:T(8,128)(2,1)S(1)}, bf16[2,512,8,128]{1,3,2,0:T(8,128)(2,1)}, u32[]{:S(2)}) copy-start(bf16[2,512,8,128]{1,3,2,0:T(8,128)(2,1)} %get-tuple-element.131) | copy-start | bytes 6291460 | tf_op jit(solution)/shard_map/while
  270.1 1.3 copy-start.7
  271.4 4.1 %copy-start.5 = (bf16[3,262144]{1,0:T(4,128)(2,1)S(1)}, bf16[3,262144]{1,0:T(4,128)(2,1)}, u32[]{:S(2)}) copy-start(bf16[3,262144]{1,0:T(4,128)(2,1)} %get-tuple-element.73) | copy-start | bytes 4718596
Sparse Core Ops, SparseCore 0:
  12.4 140.2 all-gather.1
where the time goes:
time: 287 us
  waiting for transfers between devices  142 us (49%)
  local copies, waits for them, and re-layouts  49.1 us (17%)
  other arithmetic  36.1 us (13%)
  matrix products  32.9 us (11%)
  between operations  14.2 us (5%)
  starting transfers between devices  7.51 us (3%)
  blocking collectives  4.97 us (2%)
    all_gather x1, waiting for transfers between devices, body(): gathered = lax.all_gather(master_local, 'req', axis=0, tiled=True)  142 us
    dot_general x1, matrix products, body(): jnp.dot(token_rows, gathered, preferred_element_type=jnp.float32)  17 us
    unnamed x23, local copies, waits for them, and re-layouts  16.2 us
    sub x2, other arithmetic, attend(): exp_terms = jnp.where(allowed[None], jnp.exp(scores - row_max), 0.0)  12.6 us
    dot_general x2, matrix products, attend(): jnp.einsum('htu,uhd->thd', probs, value_rows, preferred_element_type=jnp....  8.38 us
    ppermute x1, starting transfers between devices, extended(): lax.ppermute(lax.slice_in_dim(block, 0, width, axis=dim), axis, backward)  7.47 us
    dynamic_slice x6, local copies, waits for them, and re-layouts, body(): lax.map(attend, (q_rot, k_rot, v_round, lengths))  6.79 us
    convert_element_type x2, local copies, waits for them, and re-layouts, body(): rotate(key_rows.reshape(req_dev, seq_len, heads_local, HD), seq_len, HD)  6.5 us
  transfers between devices with their start and end apart: 3, of which 1 were waited for; matrix products, arithmetic and copies ran while one was open for 16% of the time, Pallas kernels for 0%

commit v1 on v0

--- a/solution.py
+++ b/solution.py
@@ -67,7 +67,9 @@
     heads_local = q_local // HD
     token_rows = tokens.reshape(req_dev * seq_len, model_width)
     master_local = qkv_master.astype(jnp.bfloat16).reshape(row_share, 3 * q_local)
-    gathered = lax.all_gather(master_local, "req", axis=0, tiled=True)
+    gathered = jnp.concatenate(
+        lax.all_to_all(jnp.stack([master_local] * lax.axis_size("req")), "req", 0, 0), axis=0
+    )
     projected = jnp.dot(token_rows, gathered, preferred_element_type=jnp.float32)
     queries = projected[:, :q_local]
     key_rows = projected[:, q_local : 2 * q_local]

time: 287 us -> 436 us (1.52); the launches traced: 287 us -> 428 us
  waiting for transfers between devices: 142 us -> 276 us
  starting transfers between devices: 7.51 us -> 23 us
  between operations: 14.2 us -> 1.04 us
  local copies, waits for them, and re-layouts: 49.1 us -> 54.5 us
    all_to_all x0 -> x1, waiting for transfers between devices: none -> 276 us  [body(): lax.all_to_all(jnp.stack([master_local] * lax.axis_size('req')), 'req', 0...]
    all_gather x1 -> x0, waiting for transfers between devices: 142 us -> none  [body(): gathered = lax.all_gather(master_local, 'req', axis=0, tiled=True)]
    all_to_all x0 -> x1, starting transfers between devices: none -> 15.5 us  [body(): lax.all_to_all(jnp.stack([master_local] * lax.axis_size('req')), 'req', 0...]
    another operation x0 -> x2, local copies, waits for them, and re-layouts: none -> 6.08 us  [body(): jnp.stack([master_local] * lax.axis_size('req'))]
    unnamed x23 -> x27, local copies, waits for them, and re-layouts: 16.2 us -> 16.1 us
  transfers between devices with their start and end apart: 3 -> 3, of which waited for: 1 -> 1; matrix products, arithmetic and copies ran while one was open for 16% -> 10% of each run, Pallas kernels for 0% -> 0%
where the time goes in v1:
time: 436 us; the launch traced here: 428 us
  waiting for transfers between devices  276 us (63%)
  local copies, waits for them, and re-layouts  54.5 us (12%)
  other arithmetic  35.6 us (8%)
  matrix products  33.1 us (8%)
  starting transfers between devices  23 us (5%)
  blocking collectives  4.97 us (1%)
    all_to_all x1, waiting for transfers between devices, body(): lax.all_to_all(jnp.stack([master_local] * lax.axis_size('req')), 'req', 0...  276 us
    dot_general x1, matrix products, body(): jnp.dot(token_rows, gathered, preferred_element_type=jnp.float32)  17 us
    unnamed x27, local copies, waits for them, and re-layouts  16.1 us
    all_to_all x1, starting transfers between devices, body(): lax.all_to_all(jnp.stack([master_local] * lax.axis_size('req')), 'req', 0...  15.5 us
    sub x2, other arithmetic, attend(): exp_terms = jnp.where(allowed[None], jnp.exp(scores - row_max), 0.0)  12.5 us
  transfers between devices with their start and end apart: 3, of which 1 were waited for; matrix products, arithmetic and copies ran while one was open for 10% of the time, Pallas kernels for 0%

profile of v1, /device:TPU:8, one launch (start us, length us, event | category | flops | bytes accessed | tf_op | source)
XLA Modules:
  0.0 428.2 jit_solution(3179558541752282364)
XLA Ops:
  0.6 0.9 convert_bitcast_fusion
  1.6 6.1 %stack.6 = bf16[128,16,3072]{2,1,0:T(8,128)(2,1)} broadcast(bf16[16,3072]{1,0:T(8,128)(2,1)S(1)} %bitcast.68), dimensions={1,2} | broadcast | bytes 12681216 | tf_op jit(solution)/shard_map/stack | solution.py:71
  7.7 15.5 %all-to-all-start = ((bf16[128,16,3072]{2,1,0:T(8,128)(2,1)}), bf16[128,16,3072]{2,1,0:T(8,128)(2,1)}, u32[]{:S(2)}, u32[]{:S(2)}) async-start(bf16[128,16,3072]{2,1,0:T(8,128)(2,1)} %stack.6), calls=%async_computation | async-start | bytes 25165824 | tf_op jit(solution)/shard_map/all_to_all | solution.py:71
  23.4 1.0 multiply_cosine_fusion
  24.4 275.7 %all-to-all-done = bf16[128,16,3072]{2,1,0:T(8,128)(2,1)} async-done(((bf16[128,16,3072]{2,1,0:T(8,128)(2,1)}), bf16[128,16,3072]{2,1,0:T(8,128)(2,1)}, u32[]{:S(2)}, u32[]{:S(2)}) %all-to-all-start) | async-done | bytes 12582944 | tf_op jit(solution)/shard_map/all_to_all | solution.py:71
  300.1 17.0 %fusion.26 = f32[1024,3072]{1,0:T(8,128)S(1)} fusion(bf16[1024,2048]{1,0:T(8,128)(2,1)} %bitcast.69, bf16[2048,3072]{1,0:T(8,128)(2,1)} %bitcast.7), kind=kOutput, calls=%fused_computation.61 | convolution fusion | flops 12884901888 | bytes 29360128 | tf_op jit(solution)/shard_map/dot_general | solution.py:73
  317.1 0.6 multiply_reduce_fusion
  318.2 3.4 copy-done.1
  322.0 1.9 copy.33
  323.9 5.0 %all-reduce = (f32[1024]{0:T(1024)S(1)}, f32[1024]{0:T(1024)S(1)}) all-reduce(f32[1024]{0:T(1024)S(1)} %get-tuple-element.48, f32[1024]{0:T(1024)S(1)} %get-tuple-element.47), channel_id=1, replica_groups=mesh['req'=128,'tp'=2] {'tp'}, use_global_device_ids=true, to_apply=%region_1.0 | all-reduce | flops 2048 | bytes 16384 | tf_op jit(solution)/shard_map/psum | solution.py:77
  328.9 5.5 %multiply_bitcast_fusion = (f32[128,8,8,128]{3,1,2,0:T(8,128)S(1)}, f32[128,8,8,128]{3,1,2,0:T(8,128)}) fusion(f32[1024,3072]{1,0:T(8,128)} %copy-done.1, f32[1024]{0:T(1024)S(1)} %copy-done.8, f32[1024]{0:T(1024)S(1)} %get-tuple-element.80, f32[1024]{0:T(1024)S(1)} %copy-done.9, f32[1024]{0:T(1024)S(1)} %get-tuple-element.81), kind=kLoop, calls=%fused_computation.32 | loop fusion | flops 4194304 | bytes 16793600
  334.4 3.0 copy.35
  337.4 2.3 stack_reshape_reshape.3
  339.7 3.2 copy.34
  342.9 4.7 %fusion.25 = (f32[2,512,8,64]{3,2,1,0:T(8,128)}, f32[2,512,8,64]{3,2,1,0:T(8,128)}) fusion(f32[2,512,8,128]{3,2,1,0:T(8,128)S(1)} %bitcast.60), kind=kLoop, calls=%fused_computation.59 | loop fusion | bytes 8388608 | tf_op jit(solution)/shard_map/slice | solution.py:35
  347.6 1.3 fusion.24
  349.0 1.7 multiply_subtract_fusion
  350.6 1.2 maximum_convert_fusion
  351.8 2.7 copy.24
  354.5 3.8 convert_element_type.79
  358.3 2.6 pad_maximum_fusion.1
  360.9 2.8 convolution_convert_fusion
  363.7 3.4 fusion.23
  367.2 1.7 copy.36
  368.9 1.7 copy.38
  370.7 7.5 %collective-permute-start = (bf16[3,2,128,1024]{3,2,1,0:T(8,128)(2,1)}, bf16[3,2,128,1024]{3,2,1,0:T(8,128)(2,1)}, u32[]{:S(2)}, u32[]{:S(2)}) collective-permute-start(bf16[3,2,128,1024]{3,2,1,0:T(8,128)(2,1)} %bitcast.25), channel_id=1, source_target_pairs={{2,0},{4,2},{6,4},{8,6},{10,8},{12,10},{14,12},{16,14},{18,16},{20... | collective-permute-start | bytes 4718600 | tf_op jit(solution)/shard_map/ppermute | solution.py:23
  378.1 1.7 subtract_convert_fusion
  379.8 2.5 pad_maximum_fusion.2
  382.3 37.2 %while.10 = (s32[]{:T(128)}, bf16[2,512,8,128]{1,3,2,0:T(8,128)(2,1)}, s32[2]{0:T(128)S(1)}, bf16[2,512,8,128]{3,2,1,0:T(8,128)(2,1)}, bf16[2,512,8,128]{3,1,2,0...) while((s32[]{:T(128)}, bf16[2,512,8,128]{1,3,2,0:T(8,128)(2,1)}, s32[2]{0:T(128)S(1)}, ...), condition=%wide.region_7.8_spmd, body=%wide.region_4.7_spmd.sunk | while | flops 1094190080 | bytes 63474368 | solution.py:88
  382.4 0.6 dynamic_slice.30
  383.0 0.6 iota_compare_fusion.5
  383.8 1.3 constant_dynamic-slice_fusion.2
  385.1 1.5 copy.48
  386.6 2.5 fusion.40
  389.1 6.3 %fusion.42 = (f32[8,512]{1,0:T(8,128)S(1)}, f32[8,512,512]{1,2,0:T(8,128)}) fusion(f32[8,512,512]{1,2,0:T(8,128)S(1)} %fusion.40, pred[512,512]{0,1:T(8,128)(4,1)S(1)} %fusion.41), kind=kOutput, calls=%fused_computation.56.clone.1 | output fusion | flops 14680575 | bytes 17055744 | tf_op jit(solution)/shard_map/while/body/eval_jaxpr/sub | solution.py:57
  395.4 4.2 fusion.43
  399.6 1.4 copy-done.7
  400.9 0.6 dynamic_slice.30
  401.6 0.6 iota_compare_fusion.5
  402.3 1.3 constant_dynamic-slice_fusion.2
  403.6 1.5 copy.48
  405.1 2.5 fusion.40
  407.6 6.3 %fusion.42 = (f32[8,512]{1,0:T(8,128)S(1)}, f32[8,512,512]{1,2,0:T(8,128)}) fusion(f32[8,512,512]{1,2,0:T(8,128)S(1)} %fusion.40, pred[512,512]{0,1:T(8,128)(4,1)S(1)} %fusion.41), kind=kOutput, calls=%fused_computation.56.clone.1 | output fusion | flops 14680575 | bytes 17055744 | tf_op jit(solution)/shard_map/while/body/eval_jaxpr/sub | solution.py:57
  413.9 4.2 fusion.43
  418.1 1.4 copy-done.7
  419.5 4.1 copy.26
  423.5 0.6 copy.37
  424.2 3.8 pad_maximum_fusion
  (44 shorter events, 1.4 us)
Async XLA Ops:
  7.7 15.5 %copy-start.10 = (s32[2,4]{1,0:T(2,128)S(1)}, s32[2,4]{1,0:T(2,128)}, u32[]{:S(2)}) copy-start(s32[2,4]{1,0:T(2,128)} %param.15) | copy-start | bytes 100
  7.7 15.5 %copy-start.11 = (s32[2,4]{1,0:T(2,128)S(1)}, s32[2,4]{1,0:T(2,128)}, u32[]{:S(2)}) copy-start(s32[2,4]{1,0:T(2,128)} %param.14) | copy-start | bytes 100
  7.7 15.5 %copy-start.12 = (s32[2]{0:T(128)S(1)}, s32[2]{0:T(128)}, u32[]{:S(2)}) copy-start(s32[2]{0:T(128)} %param.13) | copy-start | bytes 28
  7.7 292.4 %all-to-all-start = ((bf16[128,16,3072]{2,1,0:T(8,128)(2,1)}), bf16[128,16,3072]{2,1,0:T(8,128)(2,1)}, u32[]{:S(2)}, u32[]{:S(2)}) async-start(bf16[128,16,3072]{2,1,0:T(8,128)(2,1)} %stack.6), calls=%async_computation | async-start | bytes 25165824 | tf_op jit(solution)/shard_map/all_to_all | solution.py:71
  317.1 4.5 %copy-start.1 = (f32[1024,3072]{1,0:T(8,128)}, f32[1024,3072]{1,0:T(8,128)S(1)}, u32[]{:S(2)}) copy-start(f32[1024,3072]{1,0:T(8,128)S(1)} %fusion.26) | copy-start | bytes 37748740
  321.6 7.3 %copy-start.8 = (f32[1024]{0:T(1024)S(1)}, f32[1024]{0:T(1024)}, u32[]{:S(2)}) copy-start(f32[1024]{0:T(1024)} %param.12) | copy-start | bytes 12292
  321.6 7.3 %copy-start.9 = (f32[1024]{0:T(1024)S(1)}, f32[1024]{0:T(1024)}, u32[]{:S(2)}) copy-start(f32[1024]{0:T(1024)} %param.11) | copy-start | bytes 12292
  342.9 4.7 %copy-start = (f32[128,8,8,128]{3,2,1,0:T(8,128)S(1)}, f32[128,8,8,128]{3,2,1,0:T(8,128)}, u32[]{:S(2)}) copy-start(f32[128,8,8,128]{3,2,1,0:T(8,128)} %copy.35) | copy-start | bytes 12582916
  363.7 14.4 %copy-start.4 = (f32[2,512,8,64]{3,2,1,0:T(8,128)S(1)}, f32[2,512,8,64]{3,2,1,0:T(8,128)}, u32[]{:S(2)}) copy-start(f32[2,512,8,64]{3,2,1,0:T(8,128)} %get-tuple-element.77) | copy-start | bytes 6291460
  367.2 11.0 %copy-start.3 = (f32[2,512,8,64]{3,2,1,0:T(8,128)S(1)}, f32[2,512,8,64]{3,2,1,0:T(8,128)}, u32[]{:S(2)}) copy-start(f32[2,512,8,64]{3,2,1,0:T(8,128)} %get-tuple-element.76) | copy-start | bytes 6291460
  370.6 53.5 %collective-permute-start.1 = (bf16[3,2,128,1024]{3,2,1,0:T(8,128)(2,1)}, bf16[3,2,128,1024]{3,2,1,0:T(8,128)(2,1)}, u32[]{:S(2)}, u32[]{:S(2)}) collective-permute-start(bf16[3,2,128,1024]{3,2,1,0:T(8,128)(2,1)} %bitcast.31), channel_id=1, source_target_pairs={{0,2},{2,4},{4,6},{6,8},{8,10},{10,12},{12,14},{14,16},{16,18},{18... | collective-permute-start | bytes 4718600 | tf_op jit(solution)/shard_map/ppermute | solution.py:20
  370.7 53.5 %collective-permute-start = (bf16[3,2,128,1024]{3,2,1,0:T(8,128)(2,1)}, bf16[3,2,128,1024]{3,2,1,0:T(8,128)(2,1)}, u32[]{:S(2)}, u32[]{:S(2)}) collective-permute-start(bf16[3,2,128,1024]{3,2,1,0:T(8,128)(2,1)} %bitcast.25), channel_id=1, source_target_pairs={{2,0},{4,2},{6,4},{8,6},{10,8},{12,10},{14,12},{16,14},{18,16},{20... | collective-permute-start | bytes 4718600 | tf_op jit(solution)/shard_map/ppermute | solution.py:23
  389.1 6.3 %copy-start.2 = (bf16[1,512,8,128]{1,3,2,0:T(8,128)(2,1)S(1)}, bf16[1,512,8,128]{1,3,2,0:T(8,128)(2,1)}, u32[]{:S(2)}) copy-start(bf16[1,512,8,128]{1,3,2,0:T(8,128)(2,1)} %copy.48) | copy-start | bytes 3145732 | tf_op jit(solution)/shard_map/while
  389.1 6.3 %copy-start.6 = (bf16[2,512,8,128]{1,3,2,0:T(8,128)(2,1)S(1)}, bf16[2,512,8,128]{1,3,2,0:T(8,128)(2,1)}, u32[]{:S(2)}) copy-start(bf16[2,512,8,128]{1,3,2,0:T(8,128)(2,1)} %get-tuple-element.131) | copy-start | bytes 6291460 | tf_op jit(solution)/shard_map/while
  399.6 1.4 copy-start.7
  407.6 6.3 %copy-start.2 = (bf16[1,512,8,128]{1,3,2,0:T(8,128)(2,1)S(1)}, bf16[1,512,8,128]{1,3,2,0:T(8,128)(2,1)}, u32[]{:S(2)}) copy-start(bf16[1,512,8,128]{1,3,2,0:T(8,128)(2,1)} %copy.48) | copy-start | bytes 3145732 | tf_op jit(solution)/shard_map/while
  407.6 6.3 %copy-start.6 = (bf16[2,512,8,128]{1,3,2,0:T(8,128)(2,1)S(1)}, bf16[2,512,8,128]{1,3,2,0:T(8,128)(2,1)}, u32[]{:S(2)}) copy-start(bf16[2,512,8,128]{1,3,2,0:T(8,128)(2,1)} %get-tuple-element.131) | copy-start | bytes 6291460 | tf_op jit(solution)/shard_map/while
  418.1 1.4 copy-start.7
  419.5 4.1 copy-start.5
